TPU v7x, 512 devices: a whole 4x8x8 slice. The times are simulated.
512 devices in a mesh: exp: 128 (over y, z, core), hid: 4 (over x).
Axes of the slice: x: 4, y: 8, z: 8, core: 2. Of those that a mesh axis runs over, the one named last changes fastest.
Arguments:
- tokens: bfloat16 [4096, 4096], P('exp', 'hid'), may hold values from -6 to 6
- expert_ids: int32 [4096, 8], P('exp'), may hold values from 0 to 127, all different within a row; in each aligned block of 16 rows (0 to 15, 16 to 31, ...) at most 2 rows name the same one
- combine: float32 [4096, 8], P('exp'), may hold values from 0.05 to 0.4
- sign_bits: int32 [128, 768], P('exp'), may hold values from 0 to 1
- w_gate: bfloat16 [128, 768, 4096], P('exp', 'hid'), may hold values from -0.09375 to 0.09375
- w_up: bfloat16 [128, 768, 4096], P('exp', 'hid'), may hold values from -0.09375 to 0.09375
- w_down: bfloat16 [128, 768, 4096], P('exp', 'hid'), may hold values from -0.21875 to 0.21875
Outputs:
- next_input: bfloat16 [4096, 4096], P('exp', 'hid')
- hessian: bfloat16 [128, 768, 768], P('exp', 'hid')
Inputs may be any that keep to these rules, and one draw needn't show every extreme that they name: `expert_ids`: each row names 8 different experts. Within each aligned block of 16 rows (one micro-batch of one index of exp) no expert is named by more than 2 rows, a bound that some block reaches. `sign_bits`: 0 stands for the sign -1, 1 for +1.
All inputs are finite; a program needn't handle non-finite values.
Results may differ from a plain program's by a relative error of at most 0.0065.
Values may be sent and summed in bfloat16 or wider, within the bound.
No kernel may reach another device: no remote copies, remote signals or barrier semaphores. Data moves between devices by JAX's collectives and lax.ppermute only.
A program may use at most 64 MiB of HBM per device.

v0:
```python
import jax
import jax.numpy as jnp
import numpy as np
from jax import lax
from jax.sharding import PartitionSpec as P


def paley_twelve():
    residues = set((number * number % 11 for number in range(1, 11)))
    legendre = [0] + [1 if number in residues else -1 for number in range(1, 11)]
    hadamard = np.zeros((12, 12))
    hadamard[0, 1:] = 1.0
    hadamard[1:, 0] = -1.0
    for row_index in range(11):
        for col_index in range(11):
            hadamard[row_index + 1, col_index + 1] = legendre[(col_index - row_index) % 11]
    return hadamard + np.eye(12)


def sylvester(order_size):
    positions = jnp.arange(order_size, dtype=jnp.int32)
    common = positions[:, None] & positions[None, :]
    parity = jnp.zeros_like(common)
    for bit_pos in range(order_size.bit_length()):
        parity = parity + (common >> bit_pos & 1)
    return (1 - 2 * (parity % 2)).astype(jnp.float32)


def rotate(hidden, sign_rows, paley_table, sylvester_table):
    values = hidden.astype(jnp.float32) * jnp.expand_dims(sign_rows, -2)
    blocks = values.reshape(values.shape[:-1] + (12, sylvester_table.shape[0]))
    turned = jnp.einsum(
        "...ab,ca,db->...cd", blocks, paley_table, sylvester_table, precision=lax.Precision.HIGHEST
    )
    return turned.reshape(values.shape)


def rank_of_pick(ids_block, experts):
    flat_ids = ids_block.reshape(-1)
    onehot = (flat_ids[:, None] == jnp.arange(experts, dtype=jnp.int32)[None, :]).astype(jnp.int32)
    before = jnp.cumsum(onehot, axis=0) - onehot
    return jnp.sum(before * onehot, axis=1).reshape(ids_block.shape)


def local(tokens, expert_ids, combine, sign_bits, w_gate, w_up, w_down):
    n_exp = lax.axis_size("exp")
    n_hid = lax.axis_size("hid")
    hid_index = lax.axis_index("hid")
    local_experts = w_gate.shape[0]
    experts = local_experts * n_exp
    tok_rows = tokens.shape[0]
    half_rows = tok_rows // 2
    top_count = expert_ids.shape[1]
    capacity = min(half_rows, max(2, 2 * half_rows * top_count // experts))
    hidden_units = sign_bits.shape[1]
    share_rows = hidden_units // n_hid
    slot_count = n_exp * capacity
    paley_table = jnp.asarray(paley_twelve(), jnp.float32)
    sylvester_table = sylvester(hidden_units // 12)
    sign_rows = (2 * sign_bits - 1).astype(jnp.float32)
    gram_scale = experts / (tok_rows * n_exp * top_count * hidden_units)
    down_cols = lax.all_to_all(w_down, "hid", split_axis=2, concat_axis=1, tiled=True)
    gram_total = jnp.zeros((local_experts, share_rows, hidden_units), jnp.float32)
    results = []
    for batch_index in range(2):
        first_row = batch_index * half_rows
        ids_block = expert_ids[first_row : first_row + half_rows]
        picks_rank = rank_of_pick(ids_block, experts)
        target = ids_block * capacity + picks_rank
        selector = jnp.any(
            target[None, :, :] == jnp.arange(experts * capacity, dtype=jnp.int32)[:, None, None],
            axis=2,
        ).astype(jnp.bfloat16)
        sending = jnp.dot(
            selector, tokens[first_row : first_row + half_rows], preferred_element_type=jnp.float32
        ).astype(jnp.bfloat16)
        arrived = lax.all_to_all(sending, "exp", split_axis=0, concat_axis=0, tiled=True)
        arrived = lax.all_gather(arrived, "hid", axis=1, tiled=True)
        row_width = arrived.shape[1]
        expert_in = arrived.reshape(n_exp, local_experts, capacity, row_width).transpose(1, 0, 2, 3)
        expert_in = expert_in.reshape(local_experts, slot_count, row_width)
        gate_act = jnp.einsum("esd,efd->esf", expert_in, w_gate, preferred_element_type=jnp.float32)
        up_act = jnp.einsum("esd,efd->esf", expert_in, w_up, preferred_element_type=jnp.float32)
        hidden = (jax.nn.silu(gate_act) * up_act).astype(jnp.bfloat16)
        full_hidden = lax.all_gather(hidden, "hid", axis=2, tiled=True)
        summed = jnp.einsum(
            "esf,efd->esd", full_hidden, down_cols, preferred_element_type=jnp.float32
        ).astype(jnp.bfloat16)
        outgoing = summed.reshape(local_experts, n_exp, capacity, -1).transpose(1, 0, 2, 3)
        outgoing = outgoing.reshape(n_exp * local_experts * capacity, -1)
        back_rows = lax.all_to_all(outgoing, "exp", split_axis=0, concat_axis=0, tiled=True)
        picked = back_rows[target]
        weights = combine[first_row : first_row + half_rows]
        mixed_rows = tokens[first_row : first_row + half_rows].astype(jnp.float32) + jnp.sum(
            weights[:, :, None] * picked.astype(jnp.float32), axis=1
        )
        results.append(mixed_rows.astype(jnp.bfloat16))
        rotated = rotate(full_hidden, sign_rows, paley_table, sylvester_table)
        own_rotated = lax.dynamic_slice_in_dim(rotated, hid_index * share_rows, share_rows, 2)
        gram_total = gram_total + jnp.einsum(
            "esi,esj->eij", own_rotated, rotated, precision=lax.Precision.HIGHEST
        )
    hessian = (gram_total * gram_scale).astype(jnp.bfloat16)
    return (jnp.concatenate(results, axis=0), hessian)


def solution(mesh):
    placed = (
        P("exp", "hid"),
        P("exp", None),
        P("exp", None),
        P("exp", None),
        P("exp", "hid", None),
        P("exp", "hid", None),
        P("exp", "hid", None),
    )
    return jax.shard_map(
        local,
        mesh=mesh,
        in_specs=placed,
        out_specs=(P("exp", "hid"), P("exp", "hid", None)),
        check_vma=False,
    )
```

profile of v0, /device:TPU:1, one launch (start us, length us, event | category | flops | bytes accessed | tf_op | source)
XLA Modules:
  0.0 254.6 jit_solution(8127304555894847153)
XLA Ops:
  7.2 0.9 fusion.82
  8.1 0.1 copy.50
  8.2 0.1 eq.65
  8.3 0.1 fusion.40
  8.4 0.2 reduce_window_sum.18
  8.5 0.2 select_reduce_fusion
  8.7 0.1 reshape.129
  8.8 0.1 fusion.39
  9.0 1.1 convolution_convert_fusion.1
  10.1 0.2 all_to_all.52
  10.3 37.8 %all_to_all.63 = bf16[128,2,1024]{2,1,0:T(2,128)(2,1)S(1)} all-to-all(bf16[128,2,1024]{2,1,0:T(2,128)(2,1)S(1)} %all_to_all.52), channel_id=1, replica_groups=mesh['exp'=128,'hid'=4] {'exp'}, dimensions={0} | all-to-all | bytes 1048576 | tf_op jit(solution)/shard_map/all_to_all | solution.py:77
  48.0 1.0 all_to_all.54
  49.2 0.1 eq.58
  49.3 0.1 fusion.41
  49.4 0.2 reduce_window_sum.17
  49.5 0.2 select_reduce_fusion.1
  49.7 0.1 reshape.124
  49.8 0.1 fusion.38
  50.0 0.3 convolution_convert_fusion.3
  50.3 0.2 all_to_all.43
  50.5 26.2 %all_to_all.64 = bf16[128,2,1024]{2,1,0:T(2,128)(2,1)S(1)} all-to-all(bf16[128,2,1024]{2,1,0:T(2,128)(2,1)S(1)} %all_to_all.43), channel_id=1, replica_groups=mesh['exp'=128,'hid'=4] {'exp'}, dimensions={0} | all-to-all | bytes 1048576 | tf_op jit(solution)/shard_map/all_to_all | solution.py:77
  76.7 1.0 all_to_all.45
  77.7 9.9 %copy.40 = bf16[1,192,4096]{1,0,2:T(2,128)(2,1)} copy(bf16[1,192,4096]{2,1,0:T(8,128)(2,1)} %param.14) | data formatting | bytes 3145728 | tf_op args[6]
  87.6 0.5 broadcast.82
  88.1 25.0 %reduce.2 = bf16[4096,192]{1,0:T(8,128)(2,1)} reduce(bf16[4096,1,192]{2,1,0:T(2,128)(2,1)} %bitcast.77, bf16[]{:T(256)} %broadcast.82), dimensions={1}, to_apply=%bitcast.61.reduce_sub_computation | reduce | bytes 3145730
  113.1 5.0 %reshape.170 = bf16[4,2,98304]{2,1,0:T(2,128)(2,1)} reshape(bf16[4096,192]{1,0:T(8,128)(2,1)} %reduce.2) | data formatting | bytes 3145728
  118.1 4.1 %all-to-all-start.1 = ((bf16[4,2,98304]{2,1,0:T(2,128)(2,1)}), bf16[4,2,98304]{2,1,0:T(2,128)(2,1)S(1)}, u32[]{:S(2)}, u32[]{:S(2)}) async-start(bf16[4,2,98304]{2,1,0:T(2,128)(2,1)} %reshape.170), calls=%async_computation.1 | async-start | bytes 3145728 | tf_op jit(solution)/shard_map/all_to_all | solution.py:62
  122.3 0.1 reshape.149
  122.4 0.7 copy.43
  123.1 0.1 reshape.141
  123.2 0.7 copy.38
  123.9 0.6 convert_reduce_fusion
  124.5 16.4 %all-to-all-done.1 = bf16[4,2,98304]{2,1,0:T(2,128)(2,1)S(1)} async-done(((bf16[4,2,98304]{2,1,0:T(2,128)(2,1)}), bf16[4,2,98304]{2,1,0:T(2,128)(2,1)S(1)}, u32[]{:S(2)}, u32[]{:S(2)}) %all-to-all-start.1) | async-done | bytes 1572896 | tf_op jit(solution)/shard_map/all_to_all | solution.py:62
  140.9 4.1 %reshape.171 = bf16[4096,1,192]{2,1,0:T(2,128)(2,1)} reshape(bf16[4,2,98304]{2,1,0:T(2,128)(2,1)S(1)} %all-to-all-done.1) | data formatting | bytes 3145728
  145.0 9.6 %copy.41 = bf16[1,192,4096]{2,1,0:T(8,128)(2,1)} copy(bf16[1,192,4096]{1,0,2:T(2,128)(2,1)} %bitcast.78) | data formatting | bytes 3145728 | tf_op jit(solution)/shard_map/all_to_all | solution.py:62
  154.6 2.9 %all_to_all.47 = bf16[1,192,4,1024]{3,2,1,0:T(4,128)(2,1)S(1)} reshape(bf16[1,192,4096]{2,1,0:T(8,128)(2,1)} %copy.41) | data formatting | bytes 3145728 | tf_op jit(solution)/shard_map/all_to_all | solution.py:62
  157.5 1.6 copy.42
  159.1 2.6 %fusion.4 = f32[256,192]{0,1:T(8,128)S(1)} fusion(bf16[256,4096]{1,0:T(8,128)(2,1)} %all-gather.7.cloned.1.call-done, bf16[1,192,4096]{2,1,0:T(8,128)(2,1)S(1)} %copy-done), kind=kOutput, calls=%fused_computation.6 | convolution fusion | flops 402653184 | bytes 3866624 | tf_op jit(solution)/shard_map/esd,efd->esf/dot_general | solution.py:82
  161.8 0.9 fusion.17
  162.7 9.6 %all-gather.1 = bf16[256,768]{0,1:T(8,128)(2,1)S(1)} all-gather(bf16[256,192]{0,1:T(8,128)(2,1)S(1)} %fusion.17), channel_id=3, replica_groups=mesh['exp'=128,'hid'=4] {'hid'}, dimensions={1}, use_global_device_ids=true | all-gather | bytes 491520 | tf_op jit(solution)/shard_map/all_gather | solution.py:85
  172.3 1.4 convolution_convert_fusion
  173.7 2.0 all_to_all.55
  175.7 12.7 %all-to-all-start.4 = ((bf16[128,2,1024]{2,1,0:T(2,128)(2,1)}), bf16[128,2,1024]{2,1,0:T(2,128)(2,1)}, u32[]{:S(2)}, u32[]{:S(2)}) async-start(bf16[128,2,1024]{2,1,0:T(2,128)(2,1)} %all_to_all.55), calls=%async_computation.4 | async-start | bytes 1048576 | tf_op jit(solution)/shard_map/all_to_all | solution.py:91
  188.5 2.6 %fusion.6 = f32[256,192]{0,1:T(8,128)S(1)} fusion(bf16[256,4096]{1,0:T(8,128)(2,1)} %all-gather.5.cloned.1.call-done, bf16[1,192,4096]{2,1,0:T(8,128)(2,1)S(1)} %copy-done), kind=kOutput, calls=%fused_computation.8 | convolution fusion | flops 402653184 | bytes 3866624 | tf_op jit(solution)/shard_map/esd,efd->esf/dot_general | solution.py:82
  191.1 0.8 fusion.20
  192.0 10.8 %all-gather = bf16[256,768]{0,1:T(8,128)(2,1)S(1)} all-gather(bf16[256,192]{0,1:T(8,128)(2,1)S(1)} %fusion.20), channel_id=2, replica_groups=mesh['exp'=128,'hid'=4] {'hid'}, dimensions={1}, use_global_device_ids=true | all-gather | bytes 491520 | tf_op jit(solution)/shard_map/all_gather | solution.py:85
  202.8 0.7 copy-done.4
  203.6 1.4 convolution_convert_fusion.2
  205.0 2.1 all_to_all.49
  207.0 1.2 convert_multiply_fusion
  208.2 1.4 fusion.25
  209.6 15.9 %all-to-all-start.2 = ((bf16[128,2,1024]{2,1,0:T(2,128)(2,1)}), bf16[128,2,1024]{2,1,0:T(2,128)(2,1)}, u32[]{:S(2)}, u32[]{:S(2)}) async-start(bf16[128,2,1024]{2,1,0:T(2,128)(2,1)} %all_to_all.49), calls=%async_computation.2 | async-start | bytes 1048576 | tf_op jit(solution)/shard_map/all_to_all | solution.py:91
  225.5 1.3 fusion.29
  226.8 0.9 fusion.34
  227.8 1.4 fusion.23
  229.2 1.3 fusion.27
  230.5 1.7 fusion.10
  232.1 1.2 all_to_all.57
  233.4 0.9 gather_fusion.1
  234.3 10.3 %all-to-all-done.2 = bf16[128,2,1024]{2,1,0:T(2,128)(2,1)} async-done(((bf16[128,2,1024]{2,1,0:T(2,128)(2,1)}), bf16[128,2,1024]{2,1,0:T(2,128)(2,1)}, u32[]{:S(2)}, u32[]{:S(2)}) %all-to-all-start.2) | async-done | bytes 524320 | tf_op jit(solution)/shard_map/all_to_all | solution.py:91
  244.6 1.2 all_to_all.51
  245.8 0.9 gather_fusion
  246.7 0.4 fusion.31
  247.1 0.6 pad_maximum_fusion
  (41 shorter events, 0.5 us)
Async XLA Ops:
  7.2 152.0 %copy-start = (bf16[1,192,4096]{2,1,0:T(8,128)(2,1)S(1)}, bf16[1,192,4096]{2,1,0:T(8,128)(2,1)}, u32[]{:S(2)}) copy-start(bf16[1,192,4096]{2,1,0:T(8,128)(2,1)} %param.12) | copy-start | bytes 4718596
  7.2 151.9 %all-gather.7.cloned.1.call-start = ((), (), s32[]{:S(2)}) async-start(), calls=%async_computation.6 | async-start | bytes 2621440 | tf_op jit(solution)/shard_map/all_gather | solution.py:78
  10.3 39.7 %copy-start.5 = (bf16[32,1024]{1,0:T(8,128)(2,1)S(1)}, bf16[32,1024]{1,0:T(8,128)(2,1)}, u32[]{:S(2)}) copy-start(bf16[32,1024]{1,0:T(8,128)(2,1)} %param.8) | copy-start | bytes 196612
  49.1 139.4 %all-gather.5.cloned.1.call-start = ((), (), s32[]{:S(2)}) async-start(), calls=%async_computation.5 | async-start | bytes 2621440 | tf_op jit(solution)/shard_map/all_gather | solution.py:78
  118.1 4.2 %copy-start.10 = (f32[32,8]{0,1:T(8,128)S(1)}, f32[32,8]{0,1:T(8,128)}, u32[]{:S(2)}) copy-start(f32[32,8]{0,1:T(8,128)} %param.10) | copy-start | bytes 3076
  118.1 5.8 %copy-start.11 = (s32[1,768]{1,0:T(1,128)S(1)}, s32[1,768]{1,0:T(1,128)}, u32[]{:S(2)}) copy-start(s32[1,768]{1,0:T(1,128)} %param.11) | copy-start | bytes 9220
  118.1 22.8 %all-to-all-start.1 = ((bf16[4,2,98304]{2,1,0:T(2,128)(2,1)}), bf16[4,2,98304]{2,1,0:T(2,128)(2,1)S(1)}, u32[]{:S(2)}, u32[]{:S(2)}) async-start(bf16[4,2,98304]{2,1,0:T(2,128)(2,1)} %reshape.170), calls=%async_computation.1 | async-start | bytes 3145728 | tf_op jit(solution)/shard_map/all_to_all | solution.py:62
  159.1 2.6 %copy-start.1 = (bf16[256,4096]{1,0:T(8,128)(2,1)S(1)}, bf16[256,4096]{1,0:T(8,128)(2,1)}, u32[]{:S(2)}) copy-start(bf16[256,4096]{1,0:T(8,128)(2,1)} %all-gather.7.cloned.1.call-done) | copy-start | bytes 6291460
  159.1 2.7 %copy-start.12 = (bf16[1,192,4096]{2,1,0:T(8,128)(2,1)S(1)}, bf16[1,192,4096]{2,1,0:T(8,128)(2,1)}, u32[]{:S(2)}) copy-start(bf16[1,192,4096]{2,1,0:T(8,128)(2,1)} %param.13) | copy-start | bytes 4718596
  161.8 10.5 %copy-start.3 = (bf16[1,4,192,1024]{3,2,1,0:T(8,128)(2,1)S(1)}, bf16[1,4,192,1024]{3,2,1,0:T(8,128)(2,1)}, u32[]{:S(2)}) copy-start(bf16[1,4,192,1024]{3,2,1,0:T(8,128)(2,1)} %copy.42) | copy-start | bytes 4718596
  175.7 33.9 %all-to-all-start.4 = ((bf16[128,2,1024]{2,1,0:T(2,128)(2,1)}), bf16[128,2,1024]{2,1,0:T(2,128)(2,1)}, u32[]{:S(2)}, u32[]{:S(2)}) async-start(bf16[128,2,1024]{2,1,0:T(2,128)(2,1)} %all_to_all.55), calls=%async_computation.4 | async-start | bytes 1048576 | tf_op jit(solution)/shard_map/all_to_all | solution.py:91
  188.5 2.6 %copy-start.2 = (bf16[256,4096]{1,0:T(8,128)(2,1)S(1)}, bf16[256,4096]{1,0:T(8,128)(2,1)}, u32[]{:S(2)}) copy-start(bf16[256,4096]{1,0:T(8,128)(2,1)} %all-gather.5.cloned.1.call-done) | copy-start | bytes 6291460
  188.5 2.7 %copy-start.13 = (bf16[1,192,4096]{2,1,0:T(8,128)(2,1)S(1)}, bf16[1,192,4096]{2,1,0:T(8,128)(2,1)}, u32[]{:S(2)}) copy-start(bf16[1,192,4096]{2,1,0:T(8,128)(2,1)} %param.13) | copy-start | bytes 4718596
  202.8 0.7 copy-start.4
  204.9 3.3 %copy-start.7 = (f32[12,12,1]{1,0,2:T(8,128)S(1)}, f32[12,12,1]{1,0,2:T(8,128)}, u32[]{:S(2)}) copy-start(f32[12,12,1]{1,0,2:T(8,128)} %constant.69) | copy-start | bytes 1732
  209.6 35.0 %all-to-all-start.2 = ((bf16[128,2,1024]{2,1,0:T(2,128)(2,1)}), bf16[128,2,1024]{2,1,0:T(2,128)(2,1)}, u32[]{:S(2)}, u32[]{:S(2)}) async-start(bf16[128,2,1024]{2,1,0:T(2,128)(2,1)} %all_to_all.49), calls=%async_computation.2 | async-start | bytes 1048576 | tf_op jit(solution)/shard_map/all_to_all | solution.py:91
  234.2 12.4 %copy-start.8 = (f32[16,8]{1,0:T(8,128)S(1)}, f32[16,8]{1,0:T(8,128)}, u32[]{:S(2)}) copy-start(f32[16,8]{1,0:T(8,128)} %copy.43) | copy-start | bytes 1540
  234.3 12.4 %copy-start.9 = (f32[16,8]{1,0:T(8,128)S(1)}, f32[16,8]{1,0:T(8,128)}, u32[]{:S(2)}) copy-start(f32[16,8]{1,0:T(8,128)} %copy.38) | copy-start | bytes 1540
  245.8 1.3 copy-start.6
Sparse Core Ops, SparseCore 0:
  49.2 29.5 all-gather.6
  80.8 36.1 all-gather.4
where the time goes:
time: 256 us; the launch traced here: 255 us
  blocking collectives  84.4 us (33%)
  local copies, waits for them, and re-layouts  48.2 us (19%)
  starting transfers between devices  32.8 us (13%)
  other arithmetic  29 us (11%)
  waiting for transfers between devices  26.7 us (10%)
  matrix products  19.1 us (7%)
  between operations  14.4 us (6%)
    all_to_all x2, blocking collectives, local(): lax.all_to_all(sending, 'exp', split_axis=0, concat_axis=0, tiled=True)  63.9 us
    all_to_all x2, starting transfers between devices, local(): lax.all_to_all(outgoing, 'exp', split_axis=0, concat_axis=0, tiled=True)  28.6 us
    unnamed x1, other arithmetic  25 us
    unnamed x34, local copies, waits for them, and re-layouts  20.6 us
    all_gather x2, blocking collectives, local(): full_hidden = lax.all_gather(hidden, 'hid', axis=2, tiled=True)  20.5 us
    all_to_all x1, waiting for transfers between devices, local(): lax.all_to_all(w_down, 'hid', split_axis=2, concat_axis=1, tiled=True)  16.4 us
    all_to_all x3, local copies, waits for them, and re-layouts, local(): lax.all_to_all(w_down, 'hid', split_axis=2, concat_axis=1, tiled=True)  14.1 us
    all_to_all x2, waiting for transfers between devices, local(): lax.all_to_all(outgoing, 'exp', split_axis=0, concat_axis=0, tiled=True)  10.3 us
  transfers between devices with their start and end apart: 5, of which 2 were waited for; matrix products, arithmetic and copies ran while one was open for 31% of the time, Pallas kernels for 0%

commit v1 on v0

--- a/solution.py
+++ b/solution.py
@@ -3,6 +3,24 @@
 import numpy as np
 from jax import lax
 from jax.sharding import PartitionSpec as P
+
+
+def collect(array, axis, dim):
+    ways, here, hop = (lax.axis_size(axis), lax.axis_index(axis), array.shape[dim])
+    dims = [n * ways if d == dim else n for d, n in enumerate(array.shape)]
+    full = lax.dynamic_update_slice_in_dim(
+        jnp.zeros(dims, array.dtype), array, here * hop, axis=dim
+    )
+    going_up = going_down = array
+    for far in range(1, ways // 2 + 1):
+        going_up = lax.ppermute(going_up, axis, [(d, (d + 1) % ways) for d in range(ways)])
+        full = lax.dynamic_update_slice_in_dim(full, going_up, (here - far) % ways * hop, axis=dim)
+        if 2 * far < ways:
+            going_down = lax.ppermute(going_down, axis, [(d, (d - 1) % ways) for d in range(ways)])
+            full = lax.dynamic_update_slice_in_dim(
+                full, going_down, (here + far) % ways * hop, axis=dim
+            )
+    return full
 
 
 def paley_twelve():
@@ -82,7 +100,7 @@
         gate_act = jnp.einsum("esd,efd->esf", expert_in, w_gate, preferred_element_type=jnp.float32)
         up_act = jnp.einsum("esd,efd->esf", expert_in, w_up, preferred_element_type=jnp.float32)
         hidden = (jax.nn.silu(gate_act) * up_act).astype(jnp.bfloat16)
-        full_hidden = lax.all_gather(hidden, "hid", axis=2, tiled=True)
+        full_hidden = collect(hidden, "hid", 2)
         summed = jnp.einsum(
             "esf,efd->esd", full_hidden, down_cols, preferred_element_type=jnp.float32
         ).astype(jnp.bfloat16)

time: 256 us -> 246 us (0.961)
  blocking collectives: 84.4 us -> 63.9 us
  starting transfers between devices: 32.8 us -> 41.6 us
  waiting for transfers between devices: 26.7 us -> 21.9 us
  local copies, waits for them, and re-layouts: 48.2 us -> 51.6 us
    all_gather x2 -> x0, blocking collectives: 20.5 us -> none  [local(): full_hidden = lax.all_gather(hidden, 'hid', axis=2, tiled=True)]
    ppermute x0 -> x6, starting transfers between devices: none -> 17.2 us  [the longest x4 11.9 us: collect(): lax.ppermute(going_up, axis, [(d, (d + 1) % ways) for d in range(ways)])]
    all_to_all x1, waiting for transfers between devices: 16.4 us -> 0.01 us  [local(): lax.all_to_all(w_down, 'hid', split_axis=2, concat_axis=1, tiled=True)]
    all_to_all x2, waiting for transfers between devices: 10.3 us -> 21.8 us  [local(): lax.all_to_all(outgoing, 'exp', split_axis=0, concat_axis=0, tiled=True)]
    all_to_all x2, starting transfers between devices: 28.6 us -> 20.2 us  [local(): lax.all_to_all(outgoing, 'exp', split_axis=0, concat_axis=0, tiled=True)]
    dynamic_update_slice x0 -> x6, local copies, waits for them, and re-layouts: none -> 3.65 us  [the longest x4 2.73 us: collect(): lax.dynamic_update_slice_in_dim(full, going_up, (here - far) % ways * hop...]
    unnamed x34 -> x36, local copies, waits for them, and re-layouts: 20.6 us -> 21.2 us
  transfers between devices with their start and end apart: 5 -> 11, of which waited for: 2 -> 2; matrix products, arithmetic and copies ran while one was open for 31% -> 34% of each run, Pallas kernels for 0% -> 0%
where the time goes in v1:
time: 246 us; the launch traced here: 244 us
  blocking collectives  63.9 us (26%)
  local copies, waits for them, and re-layouts  51.6 us (21%)
  starting transfers between devices  41.6 us (17%)
  other arithmetic  29 us (12%)
  waiting for transfers between devices  21.9 us (9%)
  matrix products  21.3 us (9%)
  between operations  14.6 us (6%)
    all_to_all x2, blocking collectives, local(): lax.all_to_all(sending, 'exp', split_axis=0, concat_axis=0, tiled=True)  63.9 us
    unnamed x1, other arithmetic  25 us
    all_to_all x2, waiting for transfers between devices, local(): lax.all_to_all(outgoing, 'exp', split_axis=0, concat_axis=0, tiled=True)  21.8 us
    unnamed x36, local copies, waits for them, and re-layouts  21.2 us
    all_to_all x2, starting transfers between devices, local(): lax.all_to_all(outgoing, 'exp', split_axis=0, concat_axis=0, tiled=True)  20.2 us
    all_to_all x3, local copies, waits for them, and re-layouts, local(): lax.all_to_all(w_down, 'hid', split_axis=2, concat_axis=1, tiled=True)  13 us
    ppermute x4, starting transfers between devices, collect(): lax.ppermute(going_up, axis, [(d, (d + 1) % ways) for d in range(ways)])  11.9 us
    all_to_all x4, local copies, waits for them, and re-layouts, local(): lax.all_to_all(outgoing, 'exp', split_axis=0, concat_axis=0, tiled=True)  6.7 us
  transfers between devices with their start and end apart: 11, of which 2 were waited for; matrix products, arithmetic and copies ran while one was open for 34% of the time, Pallas kernels for 0%

profile of v1, /device:TPU:1, one launch (start us, length us, event | category | flops | bytes accessed | tf_op | source)
XLA Modules:
  0.0 243.8 jit_solution(7714025327580954134)
XLA Ops:
  7.2 0.9 fusion.90
  8.4 0.2 reduce_window_sum.18
  8.5 0.2 select_reduce_fusion
  8.8 0.1 fusion.47
  9.0 1.1 convolution_convert_fusion.1
  10.1 0.2 all_to_all.52
  10.3 37.8 %all_to_all.63 = bf16[128,2,1024]{2,1,0:T(2,128)(2,1)S(1)} all-to-all(bf16[128,2,1024]{2,1,0:T(2,128)(2,1)S(1)} %all_to_all.52), channel_id=1, replica_groups=mesh['exp'=128,'hid'=4] {'exp'}, dimensions={0} | all-to-all | bytes 1048576 | tf_op jit(solution)/shard_map/all_to_all | solution.py:95
  48.0 1.0 all_to_all.54
  49.4 0.2 reduce_window_sum.17
  49.5 0.2 select_reduce_fusion.1
  49.8 0.1 fusion.46
  49.9 0.3 convolution_convert_fusion.3
  50.3 0.2 all_to_all.43
  50.5 26.2 %all_to_all.64 = bf16[128,2,1024]{2,1,0:T(2,128)(2,1)S(1)} all-to-all(bf16[128,2,1024]{2,1,0:T(2,128)(2,1)S(1)} %all_to_all.43), channel_id=1, replica_groups=mesh['exp'=128,'hid'=4] {'exp'}, dimensions={0} | all-to-all | bytes 1048576 | tf_op jit(solution)/shard_map/all_to_all | solution.py:95
  76.7 1.0 all_to_all.45
  77.7 9.9 %copy.47 = bf16[1,192,4096]{1,0,2:T(2,128)(2,1)} copy(bf16[1,192,4096]{2,1,0:T(8,128)(2,1)} %param.14) | data formatting | bytes 3145728 | tf_op args[6]
  87.6 0.5 broadcast.89
  88.1 25.0 %reduce.2 = bf16[4096,192]{1,0:T(8,128)(2,1)} reduce(bf16[4096,1,192]{2,1,0:T(2,128)(2,1)} %bitcast.87, bf16[]{:T(256)} %broadcast.89), dimensions={1}, to_apply=%bitcast.69.reduce_sub_computation | reduce | bytes 3145730
  113.1 5.0 %reshape.164 = bf16[4,2,98304]{2,1,0:T(2,128)(2,1)} reshape(bf16[4096,192]{1,0:T(8,128)(2,1)} %reduce.2) | data formatting | bytes 3145728
  118.1 4.1 %all-to-all-start.1 = ((bf16[4,2,98304]{2,1,0:T(2,128)(2,1)}), bf16[4,2,98304]{2,1,0:T(2,128)(2,1)S(1)}, u32[]{:S(2)}, u32[]{:S(2)}) async-start(bf16[4,2,98304]{2,1,0:T(2,128)(2,1)} %reshape.164), calls=%async_computation.1 | async-start | bytes 3145728 | tf_op jit(solution)/shard_map/all_to_all | solution.py:80
  122.4 0.7 copy.50
  123.2 0.7 copy.45
  123.9 0.6 convert_reduce_fusion
  124.5 3.0 %fusion.4 = f32[256,192]{0,1:T(8,128)S(1)} fusion(bf16[256,4096]{1,0:T(8,128)(2,1)} %all-gather.5.cloned.1.call-done, bf16[1,192,4096]{2,1,0:T(8,128)(2,1)} %param.12), kind=kOutput, calls=%fused_computation.6 | convolution fusion | flops 402653184 | bytes 3866624 | tf_op jit(solution)/shard_map/esd,efd->esf/dot_general | solution.py:100
  127.6 1.5 constant_dynamic-update-slice_fusion.3
  129.1 0.8 copy-done.5
  129.8 3.5 %collective-permute-start.3 = (bf16[1,256,192]{1,2,0:T(8,128)(2,1)}, bf16[1,256,192]{1,2,0:T(8,128)(2,1)}, u32[]{:S(2)}, u32[]{:S(2)}) collective-permute-start(bf16[1,256,192]{1,2,0:T(8,128)(2,1)} %get-tuple-element.17), channel_id=1, source_target_pairs={{0,1},{1,2},{2,3},{3,0},{4,5},{5,6},{6,7},{7,4},{8,9},{9,10},{10,1... | collective-permute-start | bytes 294920 | tf_op jit(solution)/shard_map/ppermute | solution.py:16
  133.4 3.0 %fusion.6 = f32[256,192]{0,1:T(8,128)S(1)} fusion(bf16[256,4096]{1,0:T(8,128)(2,1)} %all-gather.3.cloned.1.call-done, bf16[1,192,4096]{2,1,0:T(8,128)(2,1)} %param.12), kind=kOutput, calls=%fused_computation.8 | convolution fusion | flops 402653184 | bytes 3866624 | tf_op jit(solution)/shard_map/esd,efd->esf/dot_general | solution.py:100
  136.5 1.5 constant_dynamic-update-slice_fusion.7
  138.0 3.1 %collective-permute-start = (bf16[1,256,192]{1,2,0:T(8,128)(2,1)}, bf16[1,256,192]{1,2,0:T(8,128)(2,1)}, u32[]{:S(2)}, u32[]{:S(2)}) collective-permute-start(bf16[1,256,192]{1,2,0:T(8,128)(2,1)} %get-tuple-element.15), channel_id=1, source_target_pairs={{0,1},{1,2},{2,3},{3,0},{4,5},{5,6},{6,7},{7,4},{8,9},{9,10},{10,1... | collective-permute-start | bytes 294920 | tf_op jit(solution)/shard_map/ppermute | solution.py:16
  141.1 4.1 %reshape.165 = bf16[4096,1,192]{2,1,0:T(2,128)(2,1)} reshape(bf16[4,2,98304]{2,1,0:T(2,128)(2,1)S(1)} %all-to-all-done.1) | data formatting | bytes 3145728
  145.2 9.7 %copy.48 = bf16[1,192,4096]{2,1,0:T(8,128)(2,1)} copy(bf16[1,192,4096]{1,0,2:T(2,128)(2,1)} %bitcast.88) | data formatting | bytes 3145728 | tf_op jit(solution)/shard_map/all_to_all | solution.py:80
  154.9 2.9 %all_to_all.47 = bf16[1,192,4,1024]{3,2,1,0:T(4,128)(2,1)S(1)} reshape(bf16[1,192,4096]{2,1,0:T(8,128)(2,1)} %copy.48) | data formatting | bytes 3145728 | tf_op jit(solution)/shard_map/all_to_all | solution.py:80
  157.8 0.5 copy.49
  158.3 3.4 %collective-permute-start.4 = (bf16[1,256,192]{1,2,0:T(8,128)(2,1)}, bf16[1,256,192]{1,2,0:T(8,128)(2,1)S(1)}, u32[]{:S(2)}, u32[]{:S(2)}) collective-permute-start(bf16[1,256,192]{1,2,0:T(8,128)(2,1)} %get-tuple-element.17), channel_id=1, source_target_pairs={{0,3},{1,0},{2,1},{3,2},{4,7},{5,4},{6,5},{7,6},{8,11},{9,8},{10,9... | collective-permute-start | bytes 294920 | tf_op jit(solution)/shard_map/ppermute | solution.py:19
  161.7 1.9 collective-permute-start.1
  163.6 3.4 %collective-permute-start.5 = (bf16[1,256,192]{1,2,0:T(8,128)(2,1)}, bf16[1,256,192]{1,2,0:T(8,128)(2,1)S(1)}, u32[]{:S(2)}, u32[]{:S(2)}) collective-permute-start(bf16[1,256,192]{1,2,0:T(8,128)(2,1)} %collective-permute-done.3), channel_id=1, source_target_pairs={{0,1},{1,2},{2,3},{3,0},{4,5},{5,6},{6,7},{7,4},{8,9},{9,10},{10,1... | collective-permute-start | bytes 294920 | tf_op jit(solution)/shard_map/ppermute | solution.py:16
  167.0 1.9 collective-permute-start.2
  169.0 0.9 constant_dynamic-update-slice_fusion.2
  169.9 0.9 constant_dynamic-update-slice_fusion.6
  170.8 0.7 copy-done.7
  171.6 1.4 convolution_convert_fusion
  173.0 2.2 all_to_all.55
  175.2 12.0 %all-to-all-start.4 = ((bf16[128,2,1024]{2,1,0:T(2,128)(2,1)}), bf16[128,2,1024]{2,1,0:T(2,128)(2,1)}, u32[]{:S(2)}, u32[]{:S(2)}) async-start(bf16[128,2,1024]{2,1,0:T(2,128)(2,1)} %all_to_all.55), calls=%async_computation.4 | async-start | bytes 1048576 | tf_op jit(solution)/shard_map/all_to_all | solution.py:109
  187.2 0.9 constant_dynamic-update-slice_fusion.5
  188.1 0.9 constant_dynamic-update-slice_fusion.4
  189.1 1.4 convolution_convert_fusion.2
  190.5 2.1 all_to_all.49
  192.5 1.2 convert_multiply_fusion
  193.7 1.4 fusion.31
  195.1 11.3 %all-to-all-done.4 = bf16[128,2,1024]{2,1,0:T(2,128)(2,1)} async-done(((bf16[128,2,1024]{2,1,0:T(2,128)(2,1)}), bf16[128,2,1024]{2,1,0:T(2,128)(2,1)}, u32[]{:S(2)}, u32[]{:S(2)}) %all-to-all-start.4) | async-done | bytes 524320 | tf_op jit(solution)/shard_map/all_to_all | solution.py:109
  206.4 8.1 %all-to-all-start.2 = ((bf16[128,2,1024]{2,1,0:T(2,128)(2,1)}), bf16[128,2,1024]{2,1,0:T(2,128)(2,1)}, u32[]{:S(2)}, u32[]{:S(2)}) async-start(bf16[128,2,1024]{2,1,0:T(2,128)(2,1)} %all_to_all.49), calls=%async_computation.2 | async-start | bytes 1048576 | tf_op jit(solution)/shard_map/all_to_all | solution.py:109
  214.6 1.3 fusion.35
  215.9 0.9 fusion.42
  216.9 1.4 fusion.29
  218.2 1.3 fusion.33
  219.6 1.7 fusion.10
  221.2 1.2 all_to_all.57
  222.5 0.9 gather_fusion.1
  223.3 10.5 %all-to-all-done.2 = bf16[128,2,1024]{2,1,0:T(2,128)(2,1)} async-done(((bf16[128,2,1024]{2,1,0:T(2,128)(2,1)}), bf16[128,2,1024]{2,1,0:T(2,128)(2,1)}, u32[]{:S(2)}, u32[]{:S(2)}) %all-to-all-start.2) | async-done | bytes 524320 | tf_op jit(solution)/shard_map/all_to_all | solution.py:109
  233.8 1.2 all_to_all.51
  235.1 0.9 gather_fusion
  235.9 0.4 fusion.37
  236.3 0.6 pad_maximum_fusion
  (61 shorter events, 1.3 us)
Async XLA Ops:
  7.2 120.4 %copy-start = (bf16[1,192,4096]{2,1,0:T(8,128)(2,1)S(1)}, bf16[1,192,4096]{2,1,0:T(8,128)(2,1)}, u32[]{:S(2)}) copy-start(bf16[1,192,4096]{2,1,0:T(8,128)(2,1)} %param.13) | copy-start | bytes 4718596
  7.2 117.3 %all-gather.5.cloned.1.call-start = ((), (), s32[]{:S(2)}) async-start(), calls=%async_computation.6 | async-start | bytes 2621440 | tf_op jit(solution)/shard_map/all_gather | solution.py:96
  10.3 39.7 %copy-start.8 = (bf16[32,1024]{1,0:T(8,128)(2,1)S(1)}, bf16[32,1024]{1,0:T(8,128)(2,1)}, u32[]{:S(2)}) copy-start(bf16[32,1024]{1,0:T(8,128)(2,1)} %param.8) | copy-start | bytes 196612
  49.1 84.3 %all-gather.3.cloned.1.call-start = ((), (), s32[]{:S(2)}) async-start(), calls=%async_computation.5 | async-start | bytes 2621440 | tf_op jit(solution)/shard_map/all_gather | solution.py:96
  118.1 4.2 %copy-start.13 = (f32[32,8]{0,1:T(8,128)S(1)}, f32[32,8]{0,1:T(8,128)}, u32[]{:S(2)}) copy-start(f32[32,8]{0,1:T(8,128)} %param.10) | copy-start | bytes 3076
  118.1 5.8 %copy-start.14 = (s32[1,768]{1,0:T(1,128)S(1)}, s32[1,768]{1,0:T(1,128)}, u32[]{:S(2)}) copy-start(s32[1,768]{1,0:T(1,128)} %param.11) | copy-start | bytes 9220
  118.1 23.0 %all-to-all-start.1 = ((bf16[4,2,98304]{2,1,0:T(2,128)(2,1)}), bf16[4,2,98304]{2,1,0:T(2,128)(2,1)S(1)}, u32[]{:S(2)}, u32[]{:S(2)}) async-start(bf16[4,2,98304]{2,1,0:T(2,128)(2,1)} %reshape.164), calls=%async_computation.1 | async-start | bytes 3145728 | tf_op jit(solution)/shard_map/all_to_all | solution.py:80
  124.5 3.1 %copy-start.1 = (bf16[256,4096]{1,0:T(8,128)(2,1)S(1)}, bf16[256,4096]{1,0:T(8,128)(2,1)}, u32[]{:S(2)}) copy-start(bf16[256,4096]{1,0:T(8,128)(2,1)} %all-gather.5.cloned.1.call-done) | copy-start | bytes 6291460
  129.1 0.8 copy-start.5
  129.8 33.8 %collective-permute-start.3 = (bf16[1,256,192]{1,2,0:T(8,128)(2,1)}, bf16[1,256,192]{1,2,0:T(8,128)(2,1)}, u32[]{:S(2)}, u32[]{:S(2)}) collective-permute-start(bf16[1,256,192]{1,2,0:T(8,128)(2,1)} %get-tuple-element.17), channel_id=1, source_target_pairs={{0,1},{1,2},{2,3},{3,0},{4,5},{5,6},{6,7},{7,4},{8,9},{9,10},{10,1... | collective-permute-start | bytes 294920 | tf_op jit(solution)/shard_map/ppermute | solution.py:16
  133.4 3.1 %copy-start.2 = (bf16[256,4096]{1,0:T(8,128)(2,1)S(1)}, bf16[256,4096]{1,0:T(8,128)(2,1)}, u32[]{:S(2)}) copy-start(bf16[256,4096]{1,0:T(8,128)(2,1)} %all-gather.3.cloned.1.call-done) | copy-start | bytes 6291460
  138.0 29.0 %collective-permute-start = (bf16[1,256,192]{1,2,0:T(8,128)(2,1)}, bf16[1,256,192]{1,2,0:T(8,128)(2,1)}, u32[]{:S(2)}, u32[]{:S(2)}) collective-permute-start(bf16[1,256,192]{1,2,0:T(8,128)(2,1)} %get-tuple-element.15), channel_id=1, source_target_pairs={{0,1},{1,2},{2,3},{3,0},{4,5},{5,6},{6,7},{7,4},{8,9},{9,10},{10,1... | collective-permute-start | bytes 294920 | tf_op jit(solution)/shard_map/ppermute | solution.py:16
  157.8 11.2 %copy-start.6 = (bf16[1,256,768]{1,2,0:T(8,128)(2,1)S(1)}, bf16[1,256,768]{1,2,0:T(8,128)(2,1)}, u32[]{:S(2)}) copy-start(bf16[1,256,768]{1,2,0:T(8,128)(2,1)} %copy-done.5) | copy-start | bytes 1179652
  158.3 12.6 %copy-start.3 = (bf16[1,4,192,1024]{3,2,1,0:T(8,128)(2,1)}, bf16[1,4,192,1024]{3,2,1,0:T(8,128)(2,1)S(1)}, u32[]{:S(2)}) copy-start(bf16[1,4,192,1024]{3,2,1,0:T(8,128)(2,1)S(1)} %copy.49) | copy-start | bytes 4718596
  158.3 12.5 %collective-permute-start.4 = (bf16[1,256,192]{1,2,0:T(8,128)(2,1)}, bf16[1,256,192]{1,2,0:T(8,128)(2,1)S(1)}, u32[]{:S(2)}, u32[]{:S(2)}) collective-permute-start(bf16[1,256,192]{1,2,0:T(8,128)(2,1)} %get-tuple-element.17), channel_id=1, source_target_pairs={{0,3},{1,0},{2,1},{3,2},{4,7},{5,4},{6,5},{7,6},{8,11},{9,8},{10,9... | collective-permute-start | bytes 294920 | tf_op jit(solution)/shard_map/ppermute | solution.py:19
  161.7 25.5 %collective-permute-start.1 = (bf16[1,256,192]{1,2,0:T(8,128)(2,1)}, bf16[1,256,192]{1,2,0:T(8,128)(2,1)}, u32[]{:S(2)}, u32[]{:S(2)}) collective-permute-start(bf16[1,256,192]{1,2,0:T(8,128)(2,1)} %get-tuple-element.15), channel_id=1, source_target_pairs={{0,3},{1,0},{2,1},{3,2},{4,7},{5,4},{6,5},{7,6},{8,11},{9,8},{10,9... | collective-permute-start | bytes 294920 | tf_op jit(solution)/shard_map/ppermute | solution.py:19
  163.6 7.2 %collective-permute-start.5 = (bf16[1,256,192]{1,2,0:T(8,128)(2,1)}, bf16[1,256,192]{1,2,0:T(8,128)(2,1)S(1)}, u32[]{:S(2)}, u32[]{:S(2)}) collective-permute-start(bf16[1,256,192]{1,2,0:T(8,128)(2,1)} %collective-permute-done.3), channel_id=1, source_target_pairs={{0,1},{1,2},{2,3},{3,0},{4,5},{5,6},{6,7},{7,4},{8,9},{9,10},{10,1... | collective-permute-start | bytes 294920 | tf_op jit(solution)/shard_map/ppermute | solution.py:16
  167.0 21.1 %collective-permute-start.2 = (bf16[1,256,192]{1,2,0:T(8,128)(2,1)}, bf16[1,256,192]{1,2,0:T(8,128)(2,1)}, u32[]{:S(2)}, u32[]{:S(2)}) collective-permute-start(bf16[1,256,192]{1,2,0:T(8,128)(2,1)} %collective-permute-done), channel_id=1, source_target_pairs={{0,1},{1,2},{2,3},{3,0},{4,5},{5,6},{6,7},{7,4},{8,9},{9,10},{10,1... | collective-permute-start | bytes 294920 | tf_op jit(solution)/shard_map/ppermute | solution.py:16
  170.8 0.8 copy-start.7
  173.0 16.1 %copy-start.4 = (bf16[1,4,192,1024]{3,2,1,0:T(8,128)(2,1)S(1)}, bf16[1,4,192,1024]{3,2,1,0:T(8,128)(2,1)}, u32[]{:S(2)}) copy-start(bf16[1,4,192,1024]{3,2,1,0:T(8,128)(2,1)} %copy-done.3) | copy-start | bytes 4718596
  175.2 31.3 %all-to-all-start.4 = ((bf16[128,2,1024]{2,1,0:T(2,128)(2,1)}), bf16[128,2,1024]{2,1,0:T(2,128)(2,1)}, u32[]{:S(2)}, u32[]{:S(2)}) async-start(bf16[128,2,1024]{2,1,0:T(2,128)(2,1)} %all_to_all.55), calls=%async_computation.4 | async-start | bytes 1048576 | tf_op jit(solution)/shard_map/all_to_all | solution.py:109
  190.5 3.2 %copy-start.10 = (f32[12,12,1]{1,0,2:T(8,128)S(1)}, f32[12,12,1]{1,0,2:T(8,128)}, u32[]{:S(2)}) copy-start(f32[12,12,1]{1,0,2:T(8,128)} %constant.99) | copy-start | bytes 1732
  206.4 27.4 %all-to-all-start.2 = ((bf16[128,2,1024]{2,1,0:T(2,128)(2,1)}), bf16[128,2,1024]{2,1,0:T(2,128)(2,1)}, u32[]{:S(2)}, u32[]{:S(2)}) async-start(bf16[128,2,1024]{2,1,0:T(2,128)(2,1)} %all_to_all.49), calls=%async_computation.2 | async-start | bytes 1048576 | tf_op jit(solution)/shard_map/all_to_all | solution.py:109
  223.3 12.6 %copy-start.11 = (f32[16,8]{1,0:T(8,128)S(1)}, f32[16,8]{1,0:T(8,128)}, u32[]{:S(2)}) copy-start(f32[16,8]{1,0:T(8,128)} %copy.50) | copy-start | bytes 1540
  223.3 12.6 %copy-start.12 = (f32[16,8]{1,0:T(8,128)S(1)}, f32[16,8]{1,0:T(8,128)}, u32[]{:S(2)}) copy-start(f32[16,8]{1,0:T(8,128)} %copy.45) | copy-start | bytes 1540
  235.0 1.3 copy-start.9
Sparse Core Ops, SparseCore 0:
  49.2 29.5 all-gather.4
  80.8 36.1 all-gather.2
